TPU v7x, 128 devices: a whole 4x4x4 slice. The times are simulated.
128 devices in a mesh: req: 4 (over z), ep: 32 (over x, y, core).
Axes of the slice: x: 4, y: 4, z: 4, core: 2. Of those that a mesh axis runs over, the one named last changes fastest.
Arguments:
- queries: bfloat16 [4096, 16, 192], P('ep'), may hold values from -260 to 260
- draft_latent: bfloat16 [4096, 576], P('ep'), may hold values from -5 to 5
- hidden_in: bfloat16 [4096, 2048], P('ep', 'req'), may hold values from -36 to 36
- cache_pool: bfloat16 [2048, 128, 576], P(('req', 'ep')), may hold values from -5 to 5
- page_table: int32 [64, 32], P('ep'), may hold values from 0 to 15, as said below
- cache_len: int32 [64], P('ep'), may hold values from 1 to 3584
- parents: int32 [64, 64], P('ep'), may hold values from -1 to 62, as said below
- accept_leaf: int32 [64], P('ep'), may hold values from 0 to 63
- absorb_key: bfloat16 [16, 128, 512], replicated, may hold values from -0.5 to 0.5
- absorb_value: bfloat16 [16, 512, 128], replicated, may hold values from -0.25 to 0.25
- out_proj: bfloat16 [2048, 2048], P(None, 'req'), may hold values from -0.125 to 0.125
- norm_gain: float32 [2048], replicated, may hold values from 0.1 to 1.9
- router: bfloat16 [2048, 64], replicated, may hold values from -0.125 to 0.125
- expert_ids: int32 [4096, 6], P('ep'), may hold values from 0 to 63, all different within a row; in each aligned block of 128 rows (0 to 127, 128 to 255, ...) at most 24 rows name the same one
- expert_gate_up: bfloat16 [64, 2, 2048, 1408], P('ep', None, None, 'req'), may hold values from -0.125 to 0.125
- expert_down: bfloat16 [64, 1408, 2048], P('ep', 'req'), may hold values from -0.15625 to 0.15625
- shared_gate_up: bfloat16 [2, 2048, 1408], P(None, None, 'req'), may hold values from -0.125 to 0.125
- shared_down: bfloat16 [1408, 2048], P('req'), may hold values from -0.15625 to 0.15625
Outputs:
- layer_out: bfloat16 [4096, 2048], P('ep', 'req')
- new_pages: bfloat16 [64, 4, 128, 576], P('ep', 'req')
Inputs may be any that keep to these rules, and one draw needn't show every extreme that they name: `page_table`: for the 2 requests of one ep index, the pages j with one value of j mod 4 name distinct slots. parents[r, i] < i, and it is -1 exactly at i = 0. `expert_ids`: in each aligned block of 128 rows no expert is named by more than 24 rows.
All inputs are finite; a program needn't handle non-finite values.
Results may differ from a plain program's by a relative error of at most 0.011.
Values may be sent and summed in bfloat16 or wider, within the bound.
No kernel may reach another device: no remote copies, remote signals or barrier semaphores. Data moves between devices by JAX's collectives and lax.ppermute only.
A program may use at most 128 MiB of HBM per device.

v0:
```python
import functools
import math

import jax
import jax.numpy as jnp
from jax import lax
from jax.experimental import pallas as pl
from jax.experimental.pallas import tpu as pltpu
from jax.sharding import PartitionSpec as P

NEGATIVE = -1e30


def ancestors(parents):
    draft_count = parents.shape[-1]
    draft_index = jnp.arange(draft_count, dtype=jnp.int32)
    ancestry = (parents[:, :, None] == draft_index[None, None, :]).astype(jnp.float32)
    ancestry = ancestry + jnp.eye(draft_count, dtype=jnp.float32)[None]
    for doubling in range(max(1, (draft_count - 1).bit_length())):
        ancestry = jnp.minimum(
            jnp.einsum("rij,rjk->rik", ancestry, ancestry, precision=lax.Precision.HIGHEST), 1.0
        )
    return ancestry


def split_exact(values):
    pieces = []
    rest = values
    for _ in range(3):
        piece = lax.reduce_precision(rest, exponent_bits=8, mantissa_bits=7)
        pieces.append(piece.astype(jnp.bfloat16))
        rest = rest - piece
    return pieces


def attention_kernel(
    slots_ref, limits_ref, q_ref, rope_ref, page_ref, draft_ref, tree_ref, mixed_ref, stats_ref,
    keys,
    *, page_size, latent_width, score_scale, row_block
):
    request = pl.program_id(0)
    page = pl.program_id(1)
    page_total = pl.num_programs(1)
    keys[page] = page_ref[0]

    @pl.when(page == page_total - 1)
    def _():
        local_pages = keys.shape[0]
        key_rows = local_pages * page_size
        column = lax.broadcasted_iota(jnp.int32, (1, key_rows), 1)
        limit = jnp.zeros((1, key_rows), jnp.int32)
        for index in range(local_pages):
            limit = jnp.where(column // page_size == index, limits_ref[request, index], limit)
        cache_ok = (column % page_size) < limit
        lane = lax.broadcasted_iota(jnp.int32, (row_block, stats_ref.shape[2]), 1)

        def body(block, carry):
            rows = pl.ds(pl.multiple_of(block * row_block, row_block), row_block)
            query = q_ref[0, rows, :]
            rope = rope_ref[0, rows, :]
            contract = (((1,), (1,)), ((), ()))
            score = jnp.concatenate(
                [
                    jnp.dot(query, keys[index, :latent_width, :], preferred_element_type=jnp.float32)
                    + jnp.dot(rope, keys[index, latent_width:, :], preferred_element_type=jnp.float32)
                    for index in range(local_pages)
                ],
                axis=1,
            ) * score_scale
            score = jnp.where(cache_ok, score, NEGATIVE)
            draft_score = (
                lax.dot_general(
                    query, draft_ref[0, :, :latent_width], contract,
                    preferred_element_type=jnp.float32,
                )
                + lax.dot_general(
                    rope, draft_ref[0, :, latent_width:], contract,
                    preferred_element_type=jnp.float32,
                )
            ) * score_scale
            tree_ok = tree_ref[0, rows, :] > 0.5
            draft_score = jnp.where(tree_ok, draft_score, NEGATIVE)
            top = jnp.maximum(
                jnp.max(score, axis=1, keepdims=True), jnp.max(draft_score, axis=1, keepdims=True)
            )
            weight = jnp.exp(score - top)
            draft_weight = jnp.exp(draft_score - top)
            total = jnp.sum(weight, axis=1, keepdims=True) + jnp.sum(
                draft_weight, axis=1, keepdims=True
            )
            weight_low = weight.astype(jnp.bfloat16)
            mixed = jnp.dot(
                draft_weight.astype(jnp.bfloat16),
                draft_ref[0, :, :latent_width],
                preferred_element_type=jnp.float32,
            )
            for index in range(local_pages):
                mixed = mixed + lax.dot_general(
                    weight_low[:, index * page_size : (index + 1) * page_size],
                    keys[index, :latent_width, :],
                    contract,
                    preferred_element_type=jnp.float32,
                )
            mixed_ref[0, rows, :] = mixed
            stats_ref[0, rows, :] = jnp.where(lane == 0, top, jnp.where(lane == 1, total, 0.0))
            return carry

        lax.fori_loop(0, q_ref.shape[1] // row_block, body, 0)


def paged_attention(slots, limits, query_rows, rope_rows, cache_pool, draft_rows, tree_rows, score_scale):
    request_count, row_count, latent_width = query_rows.shape
    key_width = cache_pool.shape[1]
    rope_width = rope_rows.shape[2]
    local_pages = slots.shape[1]
    page_size = cache_pool.shape[2]
    draft_pad = draft_rows.shape[1]
    row_block = 128
    kernel = functools.partial(
        attention_kernel,
        page_size=page_size,
        latent_width=latent_width,
        score_scale=score_scale,
        row_block=row_block,
    )
    key_rows = local_pages * page_size
    flops = 2 * request_count * row_count * (key_rows + draft_pad) * (key_width + latent_width)
    cost = pl.CostEstimate(
        flops=flops,
        transcendentals=request_count * row_count * (key_rows + draft_pad),
        bytes_accessed=2 * request_count * (row_count + key_rows) * key_width
        + 4 * request_count * row_count * (latent_width + 128 + draft_pad),
    )
    grid_spec = pltpu.PrefetchScalarGridSpec(
        num_scalar_prefetch=2,
        grid=(request_count, local_pages),
        in_specs=[
            pl.BlockSpec((1, row_count, latent_width), lambda r, j, s, n: (r, 0, 0)),
            pl.BlockSpec((1, row_count, rope_width), lambda r, j, s, n: (r, 0, 0)),
            pl.BlockSpec((1, key_width, page_size), lambda r, j, s, n: (s[r, j], 0, 0)),
            pl.BlockSpec((1, draft_pad, key_width), lambda r, j, s, n: (r, 0, 0)),
            pl.BlockSpec((1, row_count, draft_pad), lambda r, j, s, n: (r, 0, 0)),
        ],
        out_specs=[
            pl.BlockSpec((1, row_count, latent_width), lambda r, j, s, n: (r, 0, 0)),
            pl.BlockSpec((1, row_count, 128), lambda r, j, s, n: (r, 0, 0)),
        ],
        scratch_shapes=[pltpu.VMEM((local_pages, key_width, page_size), jnp.bfloat16)],
    )
    return pl.pallas_call(
        kernel,
        grid_spec=grid_spec,
        out_shape=[
            jax.ShapeDtypeStruct((request_count, row_count, latent_width), jnp.float32),
            jax.ShapeDtypeStruct((request_count, row_count, 128), jnp.float32),
        ],
        compiler_params=pltpu.CompilerParams(
            dimension_semantics=("arbitrary", "arbitrary"), vmem_limit_bytes=48 * 1024 * 1024
        ),
        cost_estimate=cost,
    )(slots, limits, query_rows, rope_rows, cache_pool, draft_rows, tree_rows)


def per_device(
    queries,
    draft_latent,
    hidden_in,
    cache_pool,
    page_table,
    cache_len,
    parents,
    accept_leaf,
    absorb_key,
    absorb_value,
    out_proj,
    norm_gain,
    router,
    expert_ids,
    expert_gate_up,
    expert_down,
    shared_gate_up,
    shared_down,
):
    highest = lax.Precision.HIGHEST
    req_count = lax.axis_size("req")
    req_index = lax.axis_index("req")
    ep_count = lax.axis_size("ep")
    request_count, draft_count = parents.shape
    token_count = request_count * draft_count
    head_count = queries.shape[1]
    nope_width = absorb_key.shape[1]
    latent_width = absorb_key.shape[2]
    page_size = cache_pool.shape[1]
    key_width = cache_pool.shape[2]
    page_count = page_table.shape[1]
    score_scale = 1.0 / math.sqrt(queries.shape[2])
    ancestry = ancestors(parents)
    depths = jnp.sum(ancestry, axis=2) - 1.0
    local_pages = page_count // req_count
    page_cols = req_index + req_count * jnp.arange(local_pages, dtype=jnp.int32)
    slot_rows = jnp.take(page_table, page_cols, axis=1)
    pool_slots = cache_pool.shape[0]
    slot_rows = jnp.clip(slot_rows, 0, pool_slots - 1).astype(jnp.int32)
    limits = jnp.clip(
        cache_len[:, None] - page_cols[None, :] * page_size, 0, page_size
    ).astype(jnp.int32)
    draft_share = draft_count // req_count
    draft_cols = req_index * draft_share + jnp.arange(draft_share, dtype=jnp.int32)
    own_latent = draft_latent.reshape(request_count, draft_count, key_width)
    draft_keys = jnp.take(own_latent, draft_cols, axis=1)
    draft_pad = 128
    draft_rows = jnp.pad(draft_keys, ((0, 0), (0, draft_pad - draft_share), (0, 0)))
    tree_ok = (jnp.take(ancestry, draft_cols, axis=2) > 0.5).astype(jnp.float32)
    tree_rows = jnp.broadcast_to(
        tree_ok[:, :, None, :], (request_count, draft_count, head_count, draft_share)
    ).reshape(request_count, draft_count * head_count, draft_share)
    tree_rows = jnp.pad(tree_rows, ((0, 0), (0, 0), (0, draft_pad - draft_share)))
    absorbed = jnp.einsum(
        "thd,hdl->thl", queries[:, :, :nope_width], absorb_key, preferred_element_type=jnp.float32
    ).astype(jnp.bfloat16)
    query_rows = absorbed.reshape(request_count, draft_count * head_count, latent_width)
    rope_rows = queries[:, :, nope_width:].reshape(request_count, draft_count * head_count, -1)
    mixed_rows, stats = paged_attention(
        slot_rows, limits, query_rows, rope_rows, jnp.swapaxes(cache_pool, 1, 2), draft_rows,
        tree_rows, score_scale,
    )
    mixed_latent = mixed_rows.reshape(request_count, draft_count, head_count, latent_width)
    highest_score = stats[:, :, 0].reshape(request_count, draft_count, head_count)
    totals = stats[:, :, 1].reshape(request_count, draft_count, head_count)
    partial_head = jnp.einsum(
        "rthl,hlv->rthv",
        mixed_latent.astype(jnp.bfloat16),
        absorb_value,
        preferred_element_type=jnp.float32,
    )
    head_width = head_count * partial_head.shape[-1]
    low_parts = split_exact(jnp.concatenate([highest_score, totals], axis=-1))
    packed = jnp.concatenate(
        [partial_head.reshape(token_count, head_width).astype(jnp.bfloat16)]
        + [part.reshape(token_count, 2 * head_count) for part in low_parts],
        axis=1,
    )
    gathered = lax.all_gather(packed, "req").astype(jnp.float32)
    part_heads = gathered[:, :, :head_width]
    rejoined = sum(
        gathered[:, :, head_width + 2 * head_count * k : head_width + 2 * head_count * (k + 1)]
        for k in range(3)
    )
    part_max = rejoined[:, :, :head_count]
    part_sum = rejoined[:, :, head_count:]
    top = jnp.max(part_max, axis=0)
    factor = jnp.exp(part_max - top[None])
    merged_sum = jnp.sum(factor * part_sum, axis=0)
    value_width = head_width // head_count
    spread = (
        jnp.arange(head_width, dtype=jnp.int32)[None, :] // value_width
        == jnp.arange(head_count, dtype=jnp.int32)[:, None]
    ).astype(jnp.bfloat16)
    scale_rows = (factor / merged_sum[None]).reshape(req_count * token_count, head_count)
    scale_high = scale_rows.astype(jnp.bfloat16)
    scale_low = (scale_rows - scale_high.astype(jnp.float32)).astype(jnp.bfloat16)
    factor_wide = (
        jnp.dot(scale_high, spread, preferred_element_type=jnp.float32)
        + jnp.dot(scale_low, spread, preferred_element_type=jnp.float32)
    ).reshape(req_count, token_count, head_width)
    head_rows = jnp.sum(factor_wide * part_heads, axis=0).astype(jnp.bfloat16)
    attention = jnp.dot(head_rows, out_proj, preferred_element_type=jnp.float32)
    resid_cols = (hidden_in.astype(jnp.float32) + attention).astype(jnp.bfloat16)
    resid = lax.all_gather(resid_cols, "req", axis=1, tiled=True)
    resid_wide = resid.astype(jnp.float32)
    normed = resid_wide * lax.rsqrt(
        jnp.mean(resid_wide * resid_wide, axis=1, keepdims=True) + 1e-06
    )
    normed = (normed * norm_gain[None, :]).astype(jnp.bfloat16)
    logits = jnp.dot(normed, router, preferred_element_type=jnp.float32)
    lifted = jax.nn.sigmoid(jnp.take_along_axis(logits, expert_ids, axis=1))
    gates = lifted / jnp.sum(lifted, axis=1, keepdims=True)
    shared_gate = jnp.dot(normed, shared_gate_up[0], preferred_element_type=jnp.float32)
    shared_lift = jnp.dot(normed, shared_gate_up[1], preferred_element_type=jnp.float32)
    shared_hidden = (jax.nn.silu(shared_gate) * shared_lift).astype(jnp.bfloat16)
    shared_part = jnp.dot(shared_hidden, shared_down, preferred_element_type=jnp.float32)
    route_width = expert_ids.shape[1]
    local_experts = expert_gate_up.shape[0]
    expert_total = local_experts * ep_count
    capacity = (2 * token_count * route_width + expert_total - 1) // expert_total
    pair_experts = expert_ids.reshape(-1)
    marks = (pair_experts[:, None] == jnp.arange(expert_total, dtype=jnp.int32)[None, :]).astype(
        jnp.int32
    )
    slot_of = jnp.sum(jnp.cumsum(marks, axis=0) * marks, axis=1) - 1
    placement = (pair_experts * capacity + slot_of).reshape(token_count, route_width)
    slot_count = expert_total * capacity
    slot_index = jnp.arange(slot_count, dtype=jnp.int32)
    hits = placement[None, :, :] == slot_index[:, None, None]
    dispatch = jnp.any(hits, axis=2).astype(jnp.bfloat16)
    outgoing = jnp.dot(dispatch, normed, preferred_element_type=jnp.float32).astype(jnp.bfloat16)
    outgoing = outgoing.reshape(ep_count, local_experts, capacity, -1)
    gate_weight = expert_gate_up[:, 0]
    lift_weight = expert_gate_up[:, 1]
    incoming = lax.all_to_all(outgoing, "ep", split_axis=0, concat_axis=0, tiled=True)
    gate_value = jnp.einsum(
        "pecd,edf->pecf", incoming, gate_weight, preferred_element_type=jnp.float32
    )
    lift_value = jnp.einsum(
        "pecd,edf->pecf", incoming, lift_weight, preferred_element_type=jnp.float32
    )
    hidden_rows = (jax.nn.silu(gate_value) * lift_value).astype(jnp.bfloat16)
    feature_share = expert_down.shape[-1] // req_count
    sending = jnp.stack(
        [
            jnp.stack(
                [
                    jnp.dot(
                        hidden_rows[:, expert],
                        expert_down[expert, :, share * feature_share : (share + 1) * feature_share],
                        preferred_element_type=jnp.float32,
                    ).astype(jnp.bfloat16)
                    for expert in range(local_experts)
                ],
                axis=1,
            )
            for share in range(req_count)
        ],
        axis=0,
    ).reshape(req_count * ep_count, local_experts, capacity, feature_share)
    returned = lax.all_to_all(sending, ("req", "ep"), 0, 0, tiled=True).reshape(
        req_count * slot_count, feature_share
    )
    combine = jnp.sum(
        jnp.where(
            placement[:, :, None] == slot_index[None, None, :], gates[:, :, None], 0.0
        ),
        axis=1,
    )
    combine = jnp.tile(combine, (1, req_count))
    combine_high = combine.astype(jnp.bfloat16)
    combine_low = (combine - combine_high.astype(jnp.float32)).astype(jnp.bfloat16)
    both = jnp.dot(
        jnp.concatenate([combine_high, combine_low], axis=0),
        returned,
        preferred_element_type=jnp.float32,
    )
    routed = both[:token_count] + both[token_count:]
    shared_cols = lax.psum_scatter(
        shared_part.astype(jnp.bfloat16), "req", scatter_dimension=1, tiled=True
    )
    layer_out = (
        resid_cols.astype(jnp.float32) + shared_cols.astype(jnp.float32) + routed
    ).astype(jnp.bfloat16)
    starts = cache_len // page_size
    page_now = starts + jnp.mod(req_index - starts, req_count)
    slot_now = jnp.take_along_axis(page_table, page_now[:, None], axis=1)[:, 0]
    old_page = cache_pool[slot_now]
    offsets = (
        page_now[:, None] * page_size
        + jnp.arange(page_size, dtype=jnp.int32)[None, :]
        - cache_len[:, None]
    ).astype(jnp.float32)
    accepted = jnp.take_along_axis(ancestry, accept_leaf[:, None, None], axis=1)[:, 0, :]
    select = accepted[:, None, :] * (depths[:, None, :] == offsets[:, :, None]).astype(jnp.float32)
    written = jnp.einsum(
        "rod,rdk->rok", select.astype(jnp.bfloat16), own_latent, preferred_element_type=jnp.float32
    )
    touched = jnp.sum(select, axis=2) > 0.5
    fresh = jnp.where(touched[..., None], written, old_page.astype(jnp.float32)).astype(
        jnp.bfloat16
    )
    return (layer_out, fresh[:, None])


def solution(mesh):
    in_specs = (
        P("ep", None, None),
        P("ep", None),
        P("ep", "req"),
        P(("req", "ep"), None, None),
        P("ep", None),
        P("ep"),
        P("ep", None),
        P("ep"),
        P(),
        P(),
        P(None, "req"),
        P(),
        P(),
        P("ep", None),
        P("ep", None, None, "req"),
        P("ep", "req", None),
        P(None, None, "req"),
        P("req", None),
    )
    out_specs = (P("ep", "req"), P("ep", "req", None, None))
    return jax.shard_map(
        per_device, mesh=mesh, in_specs=in_specs, out_specs=out_specs, check_vma=False
    )
```

profile of v0, /device:TPU:1, one launch (start us, length us, event | category | flops | bytes accessed | tf_op | source)
XLA Modules:
  0.0 301.2 jit_solution(7137555501585053611)
XLA Ops:
  7.3 0.9 copy.141
  8.8 1.8 convert_bitcast_fusion
  10.7 1.2 copy.144
  14.2 0.6 gather_fusion.1
  14.8 0.6 gather_fusion.2
  15.9 27.7 %shard_map.185 = (f32[2,1024,512]{2,1,0:T(8,128)}, f32[2,1024,128]{2,1,0:T(8,128)S(1)}) custom-call(s32[2,8]{1,0:T(2,128)S(1)} %clamp_bitcast_fusion.slots_ref, s32[2,8]{1,0:T(2,128)S(1)} %subtract_clamp_fusion.limits_ref, bf16[2,1024,512]{2,1,0:T(8,128)(2,1)S(1)} %bitcast.214, bf16[2,1024,64]{2,1,0:T(8,128)(2,1)S(1)} %bitcast.215, ...), custom_call_target="tpu_custom_call" | custom-call | flops 5133828096 | bytes 11010048 | tf_op jit(solution)/shard_map/pallas_call | solution.py:150
  43.6 2.6 convert_element_type.165
  46.5 2.5 fusion.44
  49.5 0.9 slice_reduce_fusion.1
  51.1 1.0 concatenate.19
  52.5 1.8 reduce-window.6
  55.0 0.8 fusion.4
  55.8 31.6 %all-gather.3.cloned.1.call-done = bf16[512,2144]{1,0:T(8,128)(2,1)} async-done(((bf16[128,2144]{1,0:T(8,128)(2,1)}), bf16[512,2144]{1,0:T(8,128)(2,1)}) %all-gather.3.cloned.1.call-update) | async-done | bytes 2195472 | tf_op jit(solution)/shard_map/all_gather | solution.py:243
  87.4 1.9 bitcast_convert_fusion.1
  89.8 0.7 fusion.94
  90.5 0.7 convolution_add_fusion
  91.2 0.7 fusion.5
  91.9 0.9 copy-done.3
  93.3 9.9 %all_gather.11 = bf16[128,2048]{1,0:T(8,128)(2,1)S(1)} all-gather(bf16[128,512]{1,0:T(8,128)(2,1)S(1)} %fusion.51), channel_id=1, replica_groups=mesh['req'=4,'ep'=32] {'req'}, dimensions={1}, use_global_device_ids=true | all-gather | bytes 655360 | tf_op jit(solution)/shard_map/all_gather | solution.py:269
  103.4 1.9 convolution_convert_fusion
  105.3 84.4 %all_to_all.10 = bf16[32,2,24,2048]{3,2,1,0:T(8,128)(2,1)S(1)} all-to-all(bf16[32,2,24,2048]{3,2,1,0:T(8,128)(2,1)S(1)} %bitcast.216), channel_id=1, replica_groups=mesh['req'=4,'ep'=32] {'ep'}, dimensions={0} | all-to-all | bytes 12582912 | tf_op jit(solution)/shard_map/all_to_all | solution.py:300
  189.7 3.5 %fusion.2 = f32[2,32,24,352]{3,2,1,0:T(8,128)S(1)} fusion(bf16[32,2,24,2048]{3,2,1,0:T(8,128)(2,1)S(1)} %all_to_all.10, bf16[2,2,2048,352]{2,3,1,0:T(8,128)(2,1)S(1)} %bitcast.232), kind=kOutput, calls=%fused_computation.11 | convolution fusion | flops 2214592512 | bytes 11337728 | tf_op jit(solution)/shard_map/pecd,edf->pecf/dot_general | solution.py:301
  193.2 3.7 %fusion.14 = bf16[32,2,24,352]{3,2,0,1:T(8,128)(2,1)S(1)} fusion(f32[2,32,24,352]{3,2,1,0:T(8,128)S(1)} %fusion.2, bf16[2,2,2048,352]{2,3,1,0:T(8,128)(2,1)S(1)} %bitcast.232, bf16[32,2,24,2048]{3,2,1,0:T(8,128)(2,1)S(1)} %all_to_all.10), kind=kOutput, calls=%fused_computation.31 | convolution fusion | flops 2217836544 | bytes 12615680 | tf_op jit(solution)/shard_map/pecd,edf->pecf/dot_general | solution.py:304
  196.8 0.6 fusion.36
  197.4 0.6 fusion.35
  198.0 0.6 fusion.38
  198.6 0.6 fusion.37
  199.2 0.6 fusion.32
  199.8 0.6 fusion.31
  200.4 0.6 fusion.34
  201.0 0.6 fusion.33
  202.1 0.8 pad_maximum_fusion
  203.0 3.6 %copy.170 = bf16[4,32,2,24,512]{4,3,2,1,0:T(8,128)(2,1)} copy(bf16[4,32,2,24,512]{4,3,1,2,0:T(8,128)(2,1)S(1)} %pad_maximum_fusion) | data formatting | bytes 12582912 | tf_op jit(solution)/shard_map/stack | solution.py:309
  206.6 5.1 %all-to-all-start.1 = ((bf16[128,2,24,512]{3,2,1,0:T(8,128)(2,1)}), bf16[128,2,24,512]{3,2,1,0:T(8,128)(2,1)}, u32[]{:S(2)}, u32[]{:S(2)}) async-start(bf16[128,2,24,512]{3,2,1,0:T(8,128)(2,1)} %bitcast.217), calls=%async_computation.2 | async-start | bytes 12582912 | tf_op jit(solution)/shard_map/all_to_all | solution.py:326
  212.4 0.6 gather_fusion.6
  213.0 2.3 gather_fusion.3
  215.6 0.6 gather_fusion.5
  216.5 1.1 fusion.50
  217.9 5.1 %gather_fusion.4 = f32[768]{0:T(1024)S(1)} fusion(f32[128,64]{0,1:T(8,128)S(1)} %fusion.125, s32[768]{0:T(1024)S(1)} %reshape.361), kind=kCustom, calls=%fused_computation.4 | custom fusion | bytes 12288 | tf_op jit(solution)/shard_map/jit(take_along_axis)/gather | solution.py:276
  223.3 0.7 select_reduce_fusion
  224.5 2.7 copy.184
  227.2 0.6 fusion.27
  227.8 0.7 copy-done.14
  228.5 3.7 %convolution_convert_fusion.1 = bf16[128,2048]{1,0:T(8,128)(2,1)} fusion(bf16[352,2048]{1,0:T(8,128)(2,1)S(1)} %copy-done.14, bf16[2,2048,352]{1,2,0:T(8,128)(2,1)} %param.34, f32[128,352]{0,1:T(8,128)S(1)} %fusion.27, bf16[128,2048]{1,0:T(8,128)(2,1)S(1)} %all_gather.11, f32[2048]{0:T(1024)S(1)} %copy-done.7, f32[128]{0:T(128)S(1)} %add_rsqrt_fusion), kind=kOutput, calls=%fused_computation.29 | convolution fusion | flops 370679808 | bytes 4121088 | tf_op jit(solution)/shard_map/dot_general | solution.py:281
  232.3 5.0 %subtract_convert_fusion = (bf16[128,6144]{1,0:T(8,128)(2,1)}, bf16[128,6144]{1,0:T(8,128)(2,1)}) fusion(f32[128,6144]{1,0:T(8,128)} %bitcast.219), kind=kLoop, calls=%fused_computation.24 | loop fusion | flops 3145728 | bytes 6291456 | tf_op jit(solution)/shard_map/convert_element_type | solution.py:337
  237.2 49.8 %all-to-all-done.1 = bf16[128,2,24,512]{3,2,1,0:T(8,128)(2,1)} async-done(((bf16[128,2,24,512]{3,2,1,0:T(8,128)(2,1)}), bf16[128,2,24,512]{3,2,1,0:T(8,128)(2,1)}, u32[]{:S(2)}, u32[]{:S(2)}) %all-to-all-start.1) | async-done | bytes 6291488 | tf_op jit(solution)/shard_map/all_to_all | solution.py:326
  287.0 5.7 %fusion.6 = f32[256,512]{1,0:T(8,128)S(1)} fusion(bf16[6144,512]{1,0:T(8,128)(2,1)} %bitcast.63, bf16[128,6144]{1,0:T(8,128)(2,1)} %get-tuple-element.20, bf16[128,6144]{1,0:T(8,128)(2,1)} %get-tuple-element.21), kind=kOutput, calls=%fused_computation.20 | convolution fusion | flops 1616904192 | bytes 9961472 | tf_op jit(solution)/shard_map/dot_general | solution.py:338
  292.7 1.6 fusion.82
  (127 shorter events, 10.0 us)
Async XLA Ops:
  7.2 1.7 copy-start
  7.2 80.2 %all-gather.3.cloned.1.call-start = ((), (), s32[]{:S(2)}) async-start(), calls=%async_computation.4 | async-start | bytes 2785280 | tf_op jit(solution)/shard_map/all_gather | solution.py:243
  10.7 1.2 slice-start
  10.7 1.7 copy-start.4
  10.7 2.0 copy-start.9
  11.9 3.8 %copy-start.8 = (s32[2]{0:T(128)S(1)}, s32[2]{0:T(128)}, u32[]{:S(2)}) copy-start(s32[2]{0:T(128)} %param.23) | copy-start | bytes 28
  43.6 2.9 copy-start.13
  49.4 2.7 copy-start.6
  91.2 1.6 copy-start.3
  91.2 1.6 copy-start.5
  92.8 10.6 %copy-start.7 = (f32[2048]{0:T(1024)S(1)}, f32[2048]{0:T(1024)}, u32[]{:S(2)}) copy-start(f32[2048]{0:T(1024)} %param.29) | copy-start | bytes 24580
  103.4 86.3 %slice-start.1 = ((s8[5767168]{0:T(1024)(128)(4,1)}), s8[4194304]{0:T(1024)(128)(4,1)S(1)}, s32[]{:S(2)}) async-start(s8[5767168]{0:T(1024)(128)(4,1)} %bitcast.231), calls=%async_computation.6 | async-start | bytes 8388608
  105.3 84.4 %slice-start.2 = ((s8[5767168]{0:T(1024)(128)(4,1)}), s8[1572864]{0:T(1024)(128)(4,1)S(1)}, s32[]{:S(2)}) async-start(s8[5767168]{0:T(1024)(128)(4,1)} %bitcast.231), calls=%async_computation.7 | async-start | bytes 3145728
  193.2 3.7 %copy-start.11 = (bf16[2,352,2048]{2,1,0:T(8,128)(2,1)S(1)}, bf16[2,352,2048]{2,1,0:T(8,128)(2,1)}, u32[]{:S(2)}) copy-start(bf16[2,352,2048]{2,1,0:T(8,128)(2,1)} %param.33) | copy-start | bytes 8650756
  206.6 5.5 %copy-start.10 = (s32[2]{0:T(128)S(1)}, s32[2]{0:T(128)}, u32[]{:S(2)}) copy-start(s32[2]{0:T(128)} %param.25) | copy-start | bytes 28
  206.6 5.8 %copy-start.2 = (s32[2,32]{1,0:T(2,128)S(1)}, s32[2,32]{1,0:T(2,128)}, u32[]{:S(2)}) copy-start(s32[2,32]{1,0:T(2,128)} %param.22) | copy-start | bytes 772
  206.6 11.0 %copy-start.15 = (bf16[2048,64]{0,1:T(8,128)(2,1)S(1)}, bf16[2048,64]{0,1:T(8,128)(2,1)}, u32[]{:S(2)}) copy-start(bf16[2048,64]{0,1:T(8,128)(2,1)} %param.30) | copy-start | bytes 786436
  206.6 80.5 %all-to-all-start.1 = ((bf16[128,2,24,512]{3,2,1,0:T(8,128)(2,1)}), bf16[128,2,24,512]{3,2,1,0:T(8,128)(2,1)}, u32[]{:S(2)}, u32[]{:S(2)}) async-start(bf16[128,2,24,512]{3,2,1,0:T(8,128)(2,1)} %bitcast.217), calls=%async_computation.2 | async-start | bytes 12582912 | tf_op jit(solution)/shard_map/all_to_all | solution.py:326
  211.7 81.0 %reduce-scatter.2.cloned.1.call-start = ((), (), s32[]{:S(2)}) async-start(), calls=%async_computation.3 | async-start | bytes 655360 | tf_op jit(solution)/shard_map/reduce_scatter | solution.py:344
  224.5 2.7 copy-start.12
  227.2 1.4 copy-start.14
  287.0 7.3 %copy-start.1 = (bf16[16,128,512]{2,1,0:T(8,128)(2,1)S(1)}, bf16[16,128,512]{2,1,0:T(8,128)(2,1)}, u32[]{:S(2)}) copy-start(bf16[16,128,512]{2,1,0:T(8,128)(2,1)} %param.26) | copy-start | bytes 6291460
Sparse Core Ops, SparseCore 0:
  52.2 35.1 all-gather.2
  232.4 53.9 reduce-scatter.1
where the time goes:
time: 302 us; the launch traced here: 301 us
  blocking collectives  94.3 us (31%)
  waiting for transfers between devices  81.4 us (27%)
  matrix products  32.4 us (11%)
  Pallas kernels  27.7 us (9%)
  local copies, waits for them, and re-layouts  26.9 us (9%)
  other arithmetic  18.4 us (6%)
  between operations  14.8 us (5%)
  starting transfers between devices  5.21 us (2%)
    all_to_all x1, blocking collectives, per_device(): lax.all_to_all(outgoing, 'ep', split_axis=0, concat_axis=0, tiled=True)  84.4 us
    all_to_all x1, waiting for transfers between devices, per_device(): lax.all_to_all(sending, ('req', 'ep'), 0, 0, tiled=True)  49.8 us
    all_gather x1, waiting for transfers between devices, per_device(): gathered = lax.all_gather(packed, 'req').astype(jnp.float32)  31.6 us
    pallas_call x1, Pallas kernels, paged_attention(): pl.pallas_call(kernel, grid_spec=grid_spec, out_shape=[jax.ShapeDtypeStru...  27.7 us
    all_gather x1, blocking collectives, per_device(): resid = lax.all_gather(resid_cols, 'req', axis=1, tiled=True)  9.9 us
  transfers between devices with their start and end apart: 3, of which 2 were waited for; matrix products, arithmetic and copies ran while one was open for 11% of the time, Pallas kernels for 0%

commit v1 on v0

--- a/solution.py
+++ b/solution.py
@@ -257,11 +257,8 @@
         == jnp.arange(head_count, dtype=jnp.int32)[:, None]
     ).astype(jnp.bfloat16)
     scale_rows = (factor / merged_sum[None]).reshape(req_count * token_count, head_count)
-    scale_high = scale_rows.astype(jnp.bfloat16)
-    scale_low = (scale_rows - scale_high.astype(jnp.float32)).astype(jnp.bfloat16)
-    factor_wide = (
-        jnp.dot(scale_high, spread, preferred_element_type=jnp.float32)
-        + jnp.dot(scale_low, spread, preferred_element_type=jnp.float32)
+    factor_wide = jnp.dot(
+        scale_rows.astype(jnp.bfloat16), spread, preferred_element_type=jnp.float32
     ).reshape(req_count, token_count, head_width)
     head_rows = jnp.sum(factor_wide * part_heads, axis=0).astype(jnp.bfloat16)
     attention = jnp.dot(head_rows, out_proj, preferred_element_type=jnp.float32)

time: 302 us -> 300 us (level)
  no operation moved by 1% of the time
where the time goes in v1:
time: 300 us; the launch traced here: 299 us
  blocking collectives  94.1 us (31%)
  waiting for transfers between devices  81.4 us (27%)
  matrix products  31.8 us (11%)
  Pallas kernels  27.7 us (9%)
  local copies, waits for them, and re-layouts  26.8 us (9%)
  other arithmetic  17.7 us (6%)
  between operations  14.8 us (5%)
  starting transfers between devices  5.21 us (2%)
    all_to_all x1, blocking collectives, per_device(): lax.all_to_all(outgoing, 'ep', split_axis=0, concat_axis=0, tiled=True)  84.2 us
    all_to_all x1, waiting for transfers between devices, per_device(): lax.all_to_all(sending, ('req', 'ep'), 0, 0, tiled=True)  49.8 us
    all_gather x1, waiting for transfers between devices, per_device(): gathered = lax.all_gather(packed, 'req').astype(jnp.float32)  31.6 us
    pallas_call x1, Pallas kernels, paged_attention(): pl.pallas_call(kernel, grid_spec=grid_spec, out_shape=[jax.ShapeDtypeStru...  27.7 us
    all_gather x1, blocking collectives, per_device(): resid = lax.all_gather(resid_cols, 'req', axis=1, tiled=True)  9.9 us
  transfers between devices with their start and end apart: 3, of which 2 were waited for; matrix products, arithmetic and copies ran while one was open for 11% of the time, Pallas kernels for 0%

profile of v1, /device:TPU:1, one launch (start us, length us, event | category | flops | bytes accessed | tf_op | source)
XLA Modules:
  0.0 299.5 jit_solution(12560838724677949961)
XLA Ops:
  7.3 0.9 copy.143
  8.2 0.6 gather_fusion
  8.8 1.8 convert_bitcast_fusion
  10.7 1.2 copy.146
  14.2 0.6 gather_fusion.1
  14.8 0.6 gather_fusion.2
  15.9 27.7 %shard_map.185 = (f32[2,1024,512]{2,1,0:T(8,128)}, f32[2,1024,128]{2,1,0:T(8,128)S(1)}) custom-call(s32[2,8]{1,0:T(2,128)S(1)} %clamp_bitcast_fusion.slots_ref, s32[2,8]{1,0:T(2,128)S(1)} %subtract_clamp_fusion.limits_ref, bf16[2,1024,512]{2,1,0:T(8,128)(2,1)S(1)} %bitcast.208, bf16[2,1024,64]{2,1,0:T(8,128)(2,1)S(1)} %bitcast.209, ...), custom_call_target="tpu_custom_call" | custom-call | flops 5133828096 | bytes 11010048 | tf_op jit(solution)/shard_map/pallas_call | solution.py:150
  43.6 2.6 convert_element_type.160
  46.5 2.5 fusion.44
  49.5 0.9 slice_reduce_fusion.1
  51.1 1.0 concatenate.19
  52.5 1.8 reduce-window.6
  55.0 0.8 fusion.4
  55.8 31.6 %all-gather.3.cloned.1.call-done = bf16[512,2144]{1,0:T(8,128)(2,1)} async-done(((bf16[128,2144]{1,0:T(8,128)(2,1)}), bf16[512,2144]{1,0:T(8,128)(2,1)}) %all-gather.3.cloned.1.call-update) | async-done | bytes 2195472 | tf_op jit(solution)/shard_map/all_gather | solution.py:243
  87.4 1.9 bitcast_convert_fusion
  89.7 0.8 fusion.5
  90.5 0.8 copy-done.3
  91.8 9.9 %all_gather.11 = bf16[128,2048]{1,0:T(8,128)(2,1)S(1)} all-gather(bf16[128,512]{1,0:T(8,128)(2,1)S(1)} %fusion.51), channel_id=1, replica_groups=mesh['req'=4,'ep'=32] {'req'}, dimensions={1}, use_global_device_ids=true | all-gather | bytes 655360 | tf_op jit(solution)/shard_map/all_gather | solution.py:266
  101.9 1.9 convolution_convert_fusion
  103.8 84.2 %all_to_all.10 = bf16[32,2,24,2048]{3,2,1,0:T(8,128)(2,1)S(1)} all-to-all(bf16[32,2,24,2048]{3,2,1,0:T(8,128)(2,1)S(1)} %bitcast.210), channel_id=1, replica_groups=mesh['req'=4,'ep'=32] {'ep'}, dimensions={0} | all-to-all | bytes 12582912 | tf_op jit(solution)/shard_map/all_to_all | solution.py:297
  188.0 3.5 %fusion.2 = f32[2,32,24,352]{3,2,1,0:T(8,128)S(1)} fusion(bf16[32,2,24,2048]{3,2,1,0:T(8,128)(2,1)S(1)} %all_to_all.10, bf16[2,2,2048,352]{2,3,1,0:T(8,128)(2,1)S(1)} %bitcast.225), kind=kOutput, calls=%fused_computation.11 | convolution fusion | flops 2214592512 | bytes 11337728 | tf_op jit(solution)/shard_map/pecd,edf->pecf/dot_general | solution.py:298
  191.5 3.7 %fusion.14 = bf16[32,2,24,352]{3,2,0,1:T(8,128)(2,1)S(1)} fusion(f32[2,32,24,352]{3,2,1,0:T(8,128)S(1)} %fusion.2, bf16[2,2,2048,352]{2,3,1,0:T(8,128)(2,1)S(1)} %bitcast.225, bf16[32,2,24,2048]{3,2,1,0:T(8,128)(2,1)S(1)} %all_to_all.10), kind=kOutput, calls=%fused_computation.30 | convolution fusion | flops 2217836544 | bytes 12615680 | tf_op jit(solution)/shard_map/pecd,edf->pecf/dot_general | solution.py:301
  195.1 0.6 fusion.36
  195.7 0.6 fusion.35
  196.3 0.6 fusion.38
  196.9 0.6 fusion.37
  197.5 0.6 fusion.32
  198.1 0.6 fusion.31
  198.7 0.6 fusion.34
  199.3 0.6 fusion.33
  200.4 0.8 pad_maximum_fusion
  201.3 3.6 %copy.173 = bf16[4,32,2,24,512]{4,3,2,1,0:T(8,128)(2,1)} copy(bf16[4,32,2,24,512]{4,3,1,2,0:T(8,128)(2,1)S(1)} %pad_maximum_fusion) | data formatting | bytes 12582912 | tf_op jit(solution)/shard_map/stack | solution.py:306
  204.9 5.1 %all-to-all-start.1 = ((bf16[128,2,24,512]{3,2,1,0:T(8,128)(2,1)}), bf16[128,2,24,512]{3,2,1,0:T(8,128)(2,1)}, u32[]{:S(2)}, u32[]{:S(2)}) async-start(bf16[128,2,24,512]{3,2,1,0:T(8,128)(2,1)} %bitcast.211), calls=%async_computation.2 | async-start | bytes 12582912 | tf_op jit(solution)/shard_map/all_to_all | solution.py:323
  210.7 0.6 gather_fusion.6
  211.3 2.3 gather_fusion.3
  213.9 0.6 gather_fusion.5
  214.8 1.1 fusion.50
  216.2 5.1 %gather_fusion.4 = f32[768]{0:T(1024)S(1)} fusion(f32[128,64]{0,1:T(8,128)S(1)} %fusion.125, s32[768]{0:T(1024)S(1)} %reshape.356), kind=kCustom, calls=%fused_computation.4 | custom fusion | bytes 12288 | tf_op jit(solution)/shard_map/jit(take_along_axis)/gather | solution.py:273
  221.6 0.7 select_reduce_fusion
  222.3 0.5 tile.4
  222.8 2.7 copy.188
  225.5 0.6 fusion.27
  226.1 0.7 copy-done.14
  226.8 3.7 %convolution_convert_fusion.1 = bf16[128,2048]{1,0:T(8,128)(2,1)} fusion(bf16[352,2048]{1,0:T(8,128)(2,1)S(1)} %copy-done.14, bf16[2,2048,352]{1,2,0:T(8,128)(2,1)} %param.34, f32[128,352]{0,1:T(8,128)S(1)} %fusion.27, bf16[128,2048]{1,0:T(8,128)(2,1)S(1)} %all_gather.11, f32[2048]{0:T(1024)S(1)} %copy-done.7, f32[128]{0:T(128)S(1)} %add_rsqrt_fusion), kind=kOutput, calls=%fused_computation.28 | convolution fusion | flops 370679808 | bytes 4121088 | tf_op jit(solution)/shard_map/dot_general | solution.py:278
  230.6 5.0 %subtract_convert_fusion = (bf16[128,6144]{1,0:T(8,128)(2,1)}, bf16[128,6144]{1,0:T(8,128)(2,1)}) fusion(f32[128,6144]{1,0:T(8,128)} %bitcast.212), kind=kLoop, calls=%fused_computation.23 | loop fusion | flops 3145728 | bytes 6291456 | tf_op jit(solution)/shard_map/convert_element_type | solution.py:334
  235.5 49.8 %all-to-all-done.1 = bf16[128,2,24,512]{3,2,1,0:T(8,128)(2,1)} async-done(((bf16[128,2,24,512]{3,2,1,0:T(8,128)(2,1)}), bf16[128,2,24,512]{3,2,1,0:T(8,128)(2,1)}, u32[]{:S(2)}, u32[]{:S(2)}) %all-to-all-start.1) | async-done | bytes 6291488 | tf_op jit(solution)/shard_map/all_to_all | solution.py:323
  285.3 5.7 %fusion.6 = f32[256,512]{1,0:T(8,128)S(1)} fusion(bf16[6144,512]{1,0:T(8,128)(2,1)} %bitcast.62, bf16[128,6144]{1,0:T(8,128)(2,1)} %get-tuple-element.20, bf16[128,6144]{1,0:T(8,128)(2,1)} %get-tuple-element.21), kind=kOutput, calls=%fused_computation.19 | convolution fusion | flops 1616904192 | bytes 9961472 | tf_op jit(solution)/shard_map/dot_general | solution.py:335
  291.0 1.6 fusion.82
  (123 shorter events, 8.8 us)
Async XLA Ops:
  7.2 1.7 copy-start
  7.2 80.2 %all-gather.3.cloned.1.call-start = ((), (), s32[]{:S(2)}) async-start(), calls=%async_computation.4 | async-start | bytes 2785280 | tf_op jit(solution)/shard_map/all_gather | solution.py:243
  10.7 1.2 slice-start
  10.7 1.7 copy-start.4
  10.7 2.0 copy-start.9
  11.9 3.8 %copy-start.8 = (s32[2]{0:T(128)S(1)}, s32[2]{0:T(128)}, u32[]{:S(2)}) copy-start(s32[2]{0:T(128)} %param.23) | copy-start | bytes 28
  43.6 2.9 copy-start.13
  49.4 2.7 copy-start.6
  89.7 1.6 copy-start.3
  89.7 1.6 copy-start.5
  91.3 10.6 %copy-start.7 = (f32[2048]{0:T(1024)S(1)}, f32[2048]{0:T(1024)}, u32[]{:S(2)}) copy-start(f32[2048]{0:T(1024)} %param.29) | copy-start | bytes 24580
  101.9 86.1 %slice-start.1 = ((s8[5767168]{0:T(1024)(128)(4,1)}), s8[4194304]{0:T(1024)(128)(4,1)S(1)}, s32[]{:S(2)}) async-start(s8[5767168]{0:T(1024)(128)(4,1)} %bitcast.224), calls=%async_computation.6 | async-start | bytes 8388608
  103.8 84.2 %slice-start.2 = ((s8[5767168]{0:T(1024)(128)(4,1)}), s8[1572864]{0:T(1024)(128)(4,1)S(1)}, s32[]{:S(2)}) async-start(s8[5767168]{0:T(1024)(128)(4,1)} %bitcast.224), calls=%async_computation.7 | async-start | bytes 3145728
  191.4 3.7 %copy-start.11 = (bf16[2,352,2048]{2,1,0:T(8,128)(2,1)S(1)}, bf16[2,352,2048]{2,1,0:T(8,128)(2,1)}, u32[]{:S(2)}) copy-start(bf16[2,352,2048]{2,1,0:T(8,128)(2,1)} %param.33) | copy-start | bytes 8650756
  204.8 5.5 %copy-start.10 = (s32[2]{0:T(128)S(1)}, s32[2]{0:T(128)}, u32[]{:S(2)}) copy-start(s32[2]{0:T(128)} %param.25) | copy-start | bytes 28
  204.9 5.8 %copy-start.2 = (s32[2,32]{1,0:T(2,128)S(1)}, s32[2,32]{1,0:T(2,128)}, u32[]{:S(2)}) copy-start(s32[2,32]{1,0:T(2,128)} %param.22) | copy-start | bytes 772
  204.9 11.0 %copy-start.15 = (bf16[2048,64]{0,1:T(8,128)(2,1)S(1)}, bf16[2048,64]{0,1:T(8,128)(2,1)}, u32[]{:S(2)}) copy-start(bf16[2048,64]{0,1:T(8,128)(2,1)} %param.30) | copy-start | bytes 786436
  204.9 80.4 %all-to-all-start.1 = ((bf16[128,2,24,512]{3,2,1,0:T(8,128)(2,1)}), bf16[128,2,24,512]{3,2,1,0:T(8,128)(2,1)}, u32[]{:S(2)}, u32[]{:S(2)}) async-start(bf16[128,2,24,512]{3,2,1,0:T(8,128)(2,1)} %bitcast.211), calls=%async_computation.2 | async-start | bytes 12582912 | tf_op jit(solution)/shard_map/all_to_all | solution.py:323
  210.0 81.0 %reduce-scatter.2.cloned.1.call-start = ((), (), s32[]{:S(2)}) async-start(), calls=%async_computation.3 | async-start | bytes 655360 | tf_op jit(solution)/shard_map/reduce_scatter | solution.py:341
  222.8 2.7 copy-start.12
  225.5 1.4 copy-start.14
  285.3 7.3 %copy-start.1 = (bf16[16,128,512]{2,1,0:T(8,128)(2,1)S(1)}, bf16[16,128,512]{2,1,0:T(8,128)(2,1)}, u32[]{:S(2)}) copy-start(bf16[16,128,512]{2,1,0:T(8,128)(2,1)} %param.26) | copy-start | bytes 6291460
Sparse Core Ops, SparseCore 0:
  52.2 35.1 all-gather.2
  230.7 53.9 reduce-scatter.1

commit v2 on v1

--- a/solution.py
+++ b/solution.py
@@ -330,14 +330,7 @@
         axis=1,
     )
     combine = jnp.tile(combine, (1, req_count))
-    combine_high = combine.astype(jnp.bfloat16)
-    combine_low = (combine - combine_high.astype(jnp.float32)).astype(jnp.bfloat16)
-    both = jnp.dot(
-        jnp.concatenate([combine_high, combine_low], axis=0),
-        returned,
-        preferred_element_type=jnp.float32,
-    )
-    routed = both[:token_count] + both[token_count:]
+    routed = jnp.dot(combine.astype(jnp.bfloat16), returned, preferred_element_type=jnp.float32)
     shared_cols = lax.psum_scatter(
         shared_part.astype(jnp.bfloat16), "req", scatter_dimension=1, tiled=True
     )

time: 300 us -> 299 us (level)
  other arithmetic: 17.7 us -> 11.1 us
  waiting for transfers between devices: 81.4 us -> 86.9 us
    reduce_scatter x1, waiting for transfers between devices: 0.02 us -> 54.3 us  [per_device(): lax.psum_scatter(shared_part.astype(jnp.bfloat16), 'req', scatter_dimensi...]
    all_to_all x1, waiting for transfers between devices: 49.8 us -> 1.04 us  [per_device(): lax.all_to_all(sending, ('req', 'ep'), 0, 0, tiled=True)]
    convert_element_type x2 -> x0, other arithmetic: 6.59 us -> none  [the longest x1 4.97 us: per_device(): (combine - combine_high.astype(jnp.float32)).astype(jnp.bfloat16)]
  transfers between devices with their start and end apart: 3 -> 3, of which waited for: 2 -> 3; matrix products, arithmetic and copies ran while one was open for 11% -> 8% of each run, Pallas kernels for 0% -> 0%
where the time goes in v2:
time: 299 us; the launch traced here: 298 us
  blocking collectives  94.1 us (31%)
  waiting for transfers between devices  86.9 us (29%)
  matrix products  32.4 us (11%)
  Pallas kernels  27.5 us (9%)
  local copies, waits for them, and re-layouts  25.5 us (9%)
  between operations  14.8 us (5%)
  other arithmetic  11.1 us (4%)
  starting transfers between devices  5.21 us (2%)
    all_to_all x1, blocking collectives, per_device(): lax.all_to_all(outgoing, 'ep', split_axis=0, concat_axis=0, tiled=True)  84.2 us
    reduce_scatter x1, waiting for transfers between devices, per_device(): lax.psum_scatter(shared_part.astype(jnp.bfloat16), 'req', scatter_dimensi...  54.3 us
    all_gather x1, waiting for transfers between devices, per_device(): gathered = lax.all_gather(packed, 'req').astype(jnp.float32)  31.6 us
    pallas_call x1, Pallas kernels, paged_attention(): pl.pallas_call(kernel, grid_spec=grid_spec, out_shape=[jax.ShapeDtypeStru...  27.5 us
    all_gather x1, blocking collectives, per_device(): resid = lax.all_gather(resid_cols, 'req', axis=1, tiled=True)  9.9 us
  transfers between devices with their start and end apart: 3, of which 3 were waited for; matrix products, arithmetic and copies ran while one was open for 8% of the time, Pallas kernels for 0%

profile of v2, /device:TPU:1, one launch (start us, length us, event | category | flops | bytes accessed | tf_op | source)
XLA Modules:
  0.0 297.6 jit_solution(8291710416064746453)
XLA Ops:
  7.3 1.1 convolution_minimum_fusion.5
  9.7 0.6 gather_fusion.2
  10.4 1.1 copy.148
  11.7 0.6 gather_fusion.1
  12.4 0.8 copy.143
  13.2 0.6 gather_fusion
  13.8 0.8 convert_bitcast_fusion
  14.6 1.2 copy.146
  16.5 27.5 %shard_map.185 = (f32[2,1024,512]{2,1,0:T(8,128)}, f32[2,1024,128]{2,1,0:T(8,128)S(1)}) custom-call(s32[2,8]{1,0:T(2,128)S(1)} %clamp_bitcast_fusion.slots_ref, s32[2,8]{1,0:T(2,128)S(1)} %subtract_clamp_fusion.limits_ref, bf16[2,1024,512]{2,1,0:T(8,128)(2,1)S(1)} %bitcast.209, bf16[2,1024,64]{2,1,0:T(8,128)(2,1)S(1)} %bitcast.210, ...), custom_call_target="tpu_custom_call" | custom-call | flops 5133828096 | bytes 11010048 | tf_op jit(solution)/shard_map/pallas_call | solution.py:150
  44.0 0.9 slice_reduce_fusion.1
  45.7 2.6 convert_element_type.156
  48.5 2.5 fusion.40
  51.5 1.0 concatenate.16
  52.9 1.8 reduce-window.6
  55.4 0.8 fusion.4
  56.2 31.6 %all-gather.3.cloned.1.call-done = bf16[512,2144]{1,0:T(8,128)(2,1)} async-done(((bf16[128,2144]{1,0:T(8,128)(2,1)}), bf16[512,2144]{1,0:T(8,128)(2,1)}) %all-gather.3.cloned.1.call-update) | async-done | bytes 2195472 | tf_op jit(solution)/shard_map/all_gather | solution.py:243
  87.8 1.9 bitcast_convert_fusion
  90.1 0.8 fusion.5
  90.9 0.8 copy-done.3
  91.7 0.5 fusion.47
  92.2 9.9 %all_gather.11 = bf16[128,2048]{1,0:T(8,128)(2,1)S(1)} all-gather(bf16[128,512]{1,0:T(8,128)(2,1)S(1)} %fusion.47), channel_id=1, replica_groups=mesh['req'=4,'ep'=32] {'req'}, dimensions={1}, use_global_device_ids=true | all-gather | bytes 655360 | tf_op jit(solution)/shard_map/all_gather | solution.py:266
  102.3 1.9 convolution_convert_fusion
  104.2 84.2 %all_to_all.10 = bf16[32,2,24,2048]{3,2,1,0:T(8,128)(2,1)S(1)} all-to-all(bf16[32,2,24,2048]{3,2,1,0:T(8,128)(2,1)S(1)} %bitcast.211), channel_id=1, replica_groups=mesh['req'=4,'ep'=32] {'ep'}, dimensions={0} | all-to-all | bytes 12582912 | tf_op jit(solution)/shard_map/all_to_all | solution.py:297
  188.4 3.5 %fusion.2 = f32[2,32,24,352]{3,2,1,0:T(8,128)S(1)} fusion(bf16[32,2,24,2048]{3,2,1,0:T(8,128)(2,1)S(1)} %all_to_all.10, bf16[2,2,2048,352]{2,3,1,0:T(8,128)(2,1)S(1)} %bitcast.226), kind=kOutput, calls=%fused_computation.11 | convolution fusion | flops 2214592512 | bytes 11337728 | tf_op jit(solution)/shard_map/pecd,edf->pecf/dot_general | solution.py:298
  191.9 3.7 %fusion.10 = bf16[32,2,24,352]{3,2,0,1:T(8,128)(2,1)S(1)} fusion(f32[2,32,24,352]{3,2,1,0:T(8,128)S(1)} %fusion.2, bf16[2,2,2048,352]{2,3,1,0:T(8,128)(2,1)S(1)} %bitcast.226, bf16[32,2,24,2048]{3,2,1,0:T(8,128)(2,1)S(1)} %all_to_all.10), kind=kOutput, calls=%fused_computation.25 | convolution fusion | flops 2217836544 | bytes 12615680 | tf_op jit(solution)/shard_map/pecd,edf->pecf/dot_general | solution.py:301
  195.5 0.6 fusion.27
  196.1 0.6 fusion.28
  196.7 0.6 fusion.29
  197.3 0.6 fusion.30
  197.9 0.6 fusion.31
  198.5 0.6 fusion.32
  199.1 0.6 fusion.33
  199.7 0.6 fusion.34
  200.8 0.8 pad_maximum_fusion
  201.7 3.6 %copy.173 = bf16[4,32,2,24,512]{4,3,2,1,0:T(8,128)(2,1)} copy(bf16[4,32,2,24,512]{4,3,1,2,0:T(8,128)(2,1)S(1)} %pad_maximum_fusion) | data formatting | bytes 12582912 | tf_op jit(solution)/shard_map/stack | solution.py:306
  205.3 5.1 %all-to-all-start.1 = ((bf16[128,2,24,512]{3,2,1,0:T(8,128)(2,1)}), bf16[128,2,24,512]{3,2,1,0:T(8,128)(2,1)}, u32[]{:S(2)}, u32[]{:S(2)}) async-start(bf16[128,2,24,512]{3,2,1,0:T(8,128)(2,1)} %bitcast.212), calls=%async_computation.2 | async-start | bytes 12582912 | tf_op jit(solution)/shard_map/all_to_all | solution.py:323
  211.1 0.6 gather_fusion.5
  211.9 0.6 gather_fusion.6
  212.9 2.0 fusion.23
  214.9 3.8 %convolution_convert_fusion.1 = bf16[128,2048]{1,0:T(8,128)(2,1)} fusion(bf16[352,2048]{1,0:T(8,128)(2,1)S(1)} %copy-done.12, bf16[2,2048,352]{1,2,0:T(8,128)(2,1)} %param.34, f32[128,352]{0,1:T(8,128)S(1)} %fusion.23, bf16[128,2048]{1,0:T(8,128)(2,1)S(1)} %all_gather.11, f32[2048]{0:T(1024)S(1)} %copy-done.7, f32[128]{0:T(128)S(1)} %add_rsqrt_fusion), kind=kOutput, calls=%fused_computation.23 | convolution fusion | flops 370679808 | bytes 4121088 | tf_op jit(solution)/shard_map/dot_general | solution.py:278
  218.7 2.3 gather_fusion.3
  221.0 1.1 fusion.46
  222.4 5.1 %gather_fusion.4 = f32[768]{0:T(1024)S(1)} fusion(f32[128,64]{0,1:T(8,128)S(1)} %fusion.119, s32[768]{0:T(1024)S(1)} %reshape.358), kind=kCustom, calls=%fused_computation.4 | custom fusion | bytes 12288 | tf_op jit(solution)/shard_map/jit(take_along_axis)/gather | solution.py:273
  227.8 0.7 select_reduce_fusion
  228.9 1.5 copy.188
  230.4 54.3 %reduce-scatter.2.cloned.1.call-done = bf16[128,512]{1,0:T(8,128)(2,1)} async-done(((bf16[128,2048]{1,0:T(8,128)(2,1)}), bf16[128,512]{1,0:T(8,128)(2,1)}) %reduce-scatter.2.cloned.1.call-update) | async-done | bytes 131088 | tf_op jit(solution)/shard_map/reduce_scatter | solution.py:334
  284.7 1.0 all-to-all-done.1
  285.7 5.0 %fusion.48 = bf16[128,512]{1,0:T(8,128)(2,1)} fusion(bf16[128,6144]{1,0:T(8,128)(2,1)} %bitcast.213, bf16[6144,512]{1,0:T(8,128)(2,1)} %bitcast.62, bf16[128,512]{1,0:T(8,128)(2,1)} %reduce-scatter.2.cloned.1.call-done, bf16[128,512]{1,0:T(8,128)(2,1)S(1)} %fusion.47), kind=kOutput, calls=%fused_computation.71 | convolution fusion | flops 805634048 | bytes 8257536 | tf_op jit(solution)/shard_map/dot_general | solution.py:333
  (117 shorter events, 8.3 us)
Async XLA Ops:
  7.2 6.6 %copy-start = (bf16[16,128,512]{2,1,0:T(8,128)(2,1)S(1)}, bf16[16,128,512]{2,1,0:T(8,128)(2,1)}, u32[]{:S(2)}) copy-start(bf16[16,128,512]{2,1,0:T(8,128)(2,1)} %param.26) | copy-start | bytes 6291460
  7.2 6.6 %copy-start.4 = (bf16[128,16,192]{0,2,1:T(8,128)(2,1)S(1)}, bf16[128,16,192]{0,2,1:T(8,128)(2,1)}, u32[]{:S(2)}) copy-start(bf16[128,16,192]{0,2,1:T(8,128)(2,1)} %param.18) | copy-start | bytes 2359300
  7.2 80.6 %all-gather.3.cloned.1.call-start = ((), (), s32[]{:S(2)}) async-start(), calls=%async_computation.4 | async-start | bytes 2785280 | tf_op jit(solution)/shard_map/all_gather | solution.py:243
  14.6 1.2 slice-start
  15.8 0.7 copy-start.8
  45.7 2.9 copy-start.11
  51.0 1.5 copy-start.6
  90.1 1.6 copy-start.3
  90.1 1.6 copy-start.5
  91.7 10.6 %copy-start.7 = (f32[2048]{0:T(1024)S(1)}, f32[2048]{0:T(1024)}, u32[]{:S(2)}) copy-start(f32[2048]{0:T(1024)} %param.29) | copy-start | bytes 24580
  102.3 86.1 %slice-start.1 = ((s8[5767168]{0:T(1024)(128)(4,1)}), s8[4194304]{0:T(1024)(128)(4,1)S(1)}, s32[]{:S(2)}) async-start(s8[5767168]{0:T(1024)(128)(4,1)} %bitcast.225), calls=%async_computation.6 | async-start | bytes 8388608
  104.2 84.2 %slice-start.2 = ((s8[5767168]{0:T(1024)(128)(4,1)}), s8[1572864]{0:T(1024)(128)(4,1)S(1)}, s32[]{:S(2)}) async-start(s8[5767168]{0:T(1024)(128)(4,1)} %bitcast.225), calls=%async_computation.7 | async-start | bytes 3145728
  191.9 3.7 %copy-start.10 = (bf16[2,352,2048]{2,1,0:T(8,128)(2,1)S(1)}, bf16[2,352,2048]{2,1,0:T(8,128)(2,1)}, u32[]{:S(2)}) copy-start(bf16[2,352,2048]{2,1,0:T(8,128)(2,1)} %param.33) | copy-start | bytes 8650756
  205.3 5.5 %copy-start.9 = (s32[2]{0:T(128)S(1)}, s32[2]{0:T(128)}, u32[]{:S(2)}) copy-start(s32[2]{0:T(128)} %param.25) | copy-start | bytes 28
  205.3 6.7 %copy-start.2 = (s32[2,32]{1,0:T(2,128)S(1)}, s32[2,32]{1,0:T(2,128)}, u32[]{:S(2)}) copy-start(s32[2,32]{1,0:T(2,128)} %param.22) | copy-start | bytes 772
  205.3 80.4 %all-to-all-start.1 = ((bf16[128,2,24,512]{3,2,1,0:T(8,128)(2,1)}), bf16[128,2,24,512]{3,2,1,0:T(8,128)(2,1)}, u32[]{:S(2)}, u32[]{:S(2)}) async-start(bf16[128,2,24,512]{3,2,1,0:T(8,128)(2,1)} %bitcast.212), calls=%async_computation.2 | async-start | bytes 12582912 | tf_op jit(solution)/shard_map/all_to_all | solution.py:323
  210.4 4.5 %copy-start.12 = (bf16[352,2048]{1,0:T(8,128)(2,1)S(1)}, bf16[352,2048]{1,0:T(8,128)(2,1)}, u32[]{:S(2)}) copy-start(bf16[352,2048]{1,0:T(8,128)(2,1)} %param.35) | copy-start | bytes 4325380
  210.4 74.2 %reduce-scatter.2.cloned.1.call-start = ((), (), s32[]{:S(2)}) async-start(), calls=%async_computation.3 | async-start | bytes 655360 | tf_op jit(solution)/shard_map/reduce_scatter | solution.py:334
  214.9 7.1 %copy-start.13 = (bf16[2048,64]{0,1:T(8,128)(2,1)S(1)}, bf16[2048,64]{0,1:T(8,128)(2,1)}, u32[]{:S(2)}) copy-start(bf16[2048,64]{0,1:T(8,128)(2,1)} %param.30) | copy-start | bytes 786436
  285.7 5.0 %copy-start.1 = (bf16[16,128,512]{2,1,0:T(8,128)(2,1)S(1)}, bf16[16,128,512]{2,1,0:T(8,128)(2,1)}, u32[]{:S(2)}) copy-start(bf16[16,128,512]{2,1,0:T(8,128)(2,1)} %param.26) | copy-start | bytes 6291460
Sparse Core Ops, SparseCore 0:
  52.6 35.1 all-gather.2
  218.8 65.8 reduce-scatter.1

commit v3 on v1

--- a/solution.py
+++ b/solution.py
@@ -115,7 +115,7 @@
     local_pages = slots.shape[1]
     page_size = cache_pool.shape[2]
     draft_pad = draft_rows.shape[1]
-    row_block = 128
+    row_block = 256
     kernel = functools.partial(
         attention_kernel,
         page_size=page_size,

time: 300 us -> 297 us (0.990)
  Pallas kernels: 27.7 us -> 24.6 us
    pallas_call x1, Pallas kernels: 27.7 us -> 24.6 us  [paged_attention(): pl.pallas_call(kernel, grid_spec=grid_spec, out_shape=[jax.ShapeDtypeStru...]
where the time goes in v3:
time: 297 us; the launch traced here: 296 us
  blocking collectives  94.1 us (32%)
  waiting for transfers between devices  81.4 us (27%)
  matrix products  31.8 us (11%)
  local copies, waits for them, and re-layouts  26.8 us (9%)
  Pallas kernels  24.6 us (8%)
  other arithmetic  17.7 us (6%)
  between operations  14.8 us (5%)
  starting transfers between devices  5.21 us (2%)
    all_to_all x1, blocking collectives, per_device(): lax.all_to_all(outgoing, 'ep', split_axis=0, concat_axis=0, tiled=True)  84.2 us
    all_to_all x1, waiting for transfers between devices, per_device(): lax.all_to_all(sending, ('req', 'ep'), 0, 0, tiled=True)  49.8 us
    all_gather x1, waiting for transfers between devices, per_device(): gathered = lax.all_gather(packed, 'req').astype(jnp.float32)  31.5 us
    pallas_call x1, Pallas kernels, paged_attention(): pl.pallas_call(kernel, grid_spec=grid_spec, out_shape=[jax.ShapeDtypeStru...  24.6 us
    all_gather x1, blocking collectives, per_device(): resid = lax.all_gather(resid_cols, 'req', axis=1, tiled=True)  9.9 us
  transfers between devices with their start and end apart: 3, of which 2 were waited for; matrix products, arithmetic and copies ran while one was open for 11% of the time, Pallas kernels for 0%

profile of v3, /device:TPU:1, one launch (start us, length us, event | category | flops | bytes accessed | tf_op | source)
XLA Modules:
  0.0 296.3 jit_solution(10492698278586259261)
XLA Ops:
  7.3 0.9 copy.143
  8.2 0.6 gather_fusion
  8.8 1.8 convert_bitcast_fusion
  10.7 1.2 copy.146
  14.2 0.6 gather_fusion.1
  14.8 0.6 gather_fusion.2
  15.9 24.6 %shard_map.185 = (f32[2,1024,512]{2,1,0:T(8,128)}, f32[2,1024,128]{2,1,0:T(8,128)S(1)}) custom-call(s32[2,8]{1,0:T(2,128)S(1)} %clamp_bitcast_fusion.slots_ref, s32[2,8]{1,0:T(2,128)S(1)} %subtract_clamp_fusion.limits_ref, bf16[2,1024,512]{2,1,0:T(8,128)(2,1)S(1)} %bitcast.208, bf16[2,1024,64]{2,1,0:T(8,128)(2,1)S(1)} %bitcast.209, ...), custom_call_target="tpu_custom_call" | custom-call | flops 5133828096 | bytes 11010048 | tf_op jit(solution)/shard_map/pallas_call | solution.py:150
  40.5 2.6 convert_element_type.160
  43.4 2.5 fusion.44
  46.4 0.9 slice_reduce_fusion.1
  48.0 1.0 concatenate.19
  49.4 1.8 reduce-window.6
  51.9 0.8 fusion.4
  52.7 31.5 %all-gather.3.cloned.1.call-done = bf16[512,2144]{1,0:T(8,128)(2,1)} async-done(((bf16[128,2144]{1,0:T(8,128)(2,1)}), bf16[512,2144]{1,0:T(8,128)(2,1)}) %all-gather.3.cloned.1.call-update) | async-done | bytes 2195472 | tf_op jit(solution)/shard_map/all_gather | solution.py:243
  84.3 1.9 bitcast_convert_fusion
  86.6 0.8 fusion.5
  87.4 0.8 copy-done.3
  88.7 9.9 %all_gather.11 = bf16[128,2048]{1,0:T(8,128)(2,1)S(1)} all-gather(bf16[128,512]{1,0:T(8,128)(2,1)S(1)} %fusion.51), channel_id=1, replica_groups=mesh['req'=4,'ep'=32] {'req'}, dimensions={1}, use_global_device_ids=true | all-gather | bytes 655360 | tf_op jit(solution)/shard_map/all_gather | solution.py:266
  98.8 1.9 convolution_convert_fusion
  100.7 84.2 %all_to_all.10 = bf16[32,2,24,2048]{3,2,1,0:T(8,128)(2,1)S(1)} all-to-all(bf16[32,2,24,2048]{3,2,1,0:T(8,128)(2,1)S(1)} %bitcast.210), channel_id=1, replica_groups=mesh['req'=4,'ep'=32] {'ep'}, dimensions={0} | all-to-all | bytes 12582912 | tf_op jit(solution)/shard_map/all_to_all | solution.py:297
  184.9 3.5 %fusion.2 = f32[2,32,24,352]{3,2,1,0:T(8,128)S(1)} fusion(bf16[32,2,24,2048]{3,2,1,0:T(8,128)(2,1)S(1)} %all_to_all.10, bf16[2,2,2048,352]{2,3,1,0:T(8,128)(2,1)S(1)} %bitcast.225), kind=kOutput, calls=%fused_computation.11 | convolution fusion | flops 2214592512 | bytes 11337728 | tf_op jit(solution)/shard_map/pecd,edf->pecf/dot_general | solution.py:298
  188.3 3.7 %fusion.14 = bf16[32,2,24,352]{3,2,0,1:T(8,128)(2,1)S(1)} fusion(f32[2,32,24,352]{3,2,1,0:T(8,128)S(1)} %fusion.2, bf16[2,2,2048,352]{2,3,1,0:T(8,128)(2,1)S(1)} %bitcast.225, bf16[32,2,24,2048]{3,2,1,0:T(8,128)(2,1)S(1)} %all_to_all.10), kind=kOutput, calls=%fused_computation.30 | convolution fusion | flops 2217836544 | bytes 12615680 | tf_op jit(solution)/shard_map/pecd,edf->pecf/dot_general | solution.py:301
  192.0 0.6 fusion.36
  192.6 0.6 fusion.35
  193.2 0.6 fusion.38
  193.8 0.6 fusion.37
  194.4 0.6 fusion.32
  195.0 0.6 fusion.31
  195.5 0.6 fusion.34
  196.1 0.6 fusion.33
  197.3 0.8 pad_maximum_fusion
  198.1 3.6 %copy.173 = bf16[4,32,2,24,512]{4,3,2,1,0:T(8,128)(2,1)} copy(bf16[4,32,2,24,512]{4,3,1,2,0:T(8,128)(2,1)S(1)} %pad_maximum_fusion) | data formatting | bytes 12582912 | tf_op jit(solution)/shard_map/stack | solution.py:306
  201.7 5.1 %all-to-all-start.1 = ((bf16[128,2,24,512]{3,2,1,0:T(8,128)(2,1)}), bf16[128,2,24,512]{3,2,1,0:T(8,128)(2,1)}, u32[]{:S(2)}, u32[]{:S(2)}) async-start(bf16[128,2,24,512]{3,2,1,0:T(8,128)(2,1)} %bitcast.211), calls=%async_computation.2 | async-start | bytes 12582912 | tf_op jit(solution)/shard_map/all_to_all | solution.py:323
  207.6 0.6 gather_fusion.6
  208.2 2.3 gather_fusion.3
  210.8 0.6 gather_fusion.5
  211.6 1.1 fusion.50
  213.1 5.1 %gather_fusion.4 = f32[768]{0:T(1024)S(1)} fusion(f32[128,64]{0,1:T(8,128)S(1)} %fusion.125, s32[768]{0:T(1024)S(1)} %reshape.356), kind=kCustom, calls=%fused_computation.4 | custom fusion | bytes 12288 | tf_op jit(solution)/shard_map/jit(take_along_axis)/gather | solution.py:273
  218.5 0.7 select_reduce_fusion
  219.1 0.5 tile.4
  219.7 2.7 copy.188
  222.4 0.6 fusion.27
  223.0 0.7 copy-done.14
  223.7 3.7 %convolution_convert_fusion.1 = bf16[128,2048]{1,0:T(8,128)(2,1)} fusion(bf16[352,2048]{1,0:T(8,128)(2,1)S(1)} %copy-done.14, bf16[2,2048,352]{1,2,0:T(8,128)(2,1)} %param.34, f32[128,352]{0,1:T(8,128)S(1)} %fusion.27, bf16[128,2048]{1,0:T(8,128)(2,1)S(1)} %all_gather.11, f32[2048]{0:T(1024)S(1)} %copy-done.7, f32[128]{0:T(128)S(1)} %add_rsqrt_fusion), kind=kOutput, calls=%fused_computation.28 | convolution fusion | flops 370679808 | bytes 4121088 | tf_op jit(solution)/shard_map/dot_general | solution.py:278
  227.4 5.0 %subtract_convert_fusion = (bf16[128,6144]{1,0:T(8,128)(2,1)}, bf16[128,6144]{1,0:T(8,128)(2,1)}) fusion(f32[128,6144]{1,0:T(8,128)} %bitcast.212), kind=kLoop, calls=%fused_computation.23 | loop fusion | flops 3145728 | bytes 6291456 | tf_op jit(solution)/shard_map/convert_element_type | solution.py:334
  232.4 49.8 %all-to-all-done.1 = bf16[128,2,24,512]{3,2,1,0:T(8,128)(2,1)} async-done(((bf16[128,2,24,512]{3,2,1,0:T(8,128)(2,1)}), bf16[128,2,24,512]{3,2,1,0:T(8,128)(2,1)}, u32[]{:S(2)}, u32[]{:S(2)}) %all-to-all-start.1) | async-done | bytes 6291488 | tf_op jit(solution)/shard_map/all_to_all | solution.py:323
  282.2 5.7 %fusion.6 = f32[256,512]{1,0:T(8,128)S(1)} fusion(bf16[6144,512]{1,0:T(8,128)(2,1)} %bitcast.62, bf16[128,6144]{1,0:T(8,128)(2,1)} %get-tuple-element.20, bf16[128,6144]{1,0:T(8,128)(2,1)} %get-tuple-element.21), kind=kOutput, calls=%fused_computation.19 | convolution fusion | flops 1616904192 | bytes 9961472 | tf_op jit(solution)/shard_map/dot_general | solution.py:335
  287.9 1.6 fusion.82
  (123 shorter events, 8.8 us)
Async XLA Ops:
  7.2 1.7 copy-start
  7.2 77.1 %all-gather.3.cloned.1.call-start = ((), (), s32[]{:S(2)}) async-start(), calls=%async_computation.4 | async-start | bytes 2785280 | tf_op jit(solution)/shard_map/all_gather | solution.py:243
  10.7 1.2 slice-start
  10.7 1.7 copy-start.4
  10.7 2.0 copy-start.9
  11.9 3.8 %copy-start.8 = (s32[2]{0:T(128)S(1)}, s32[2]{0:T(128)}, u32[]{:S(2)}) copy-start(s32[2]{0:T(128)} %param.23) | copy-start | bytes 28
  40.5 2.9 copy-start.13
  46.3 2.7 copy-start.6
  86.6 1.6 copy-start.3
  86.6 1.6 copy-start.5
  88.2 10.6 %copy-start.7 = (f32[2048]{0:T(1024)S(1)}, f32[2048]{0:T(1024)}, u32[]{:S(2)}) copy-start(f32[2048]{0:T(1024)} %param.29) | copy-start | bytes 24580
  98.8 86.1 %slice-start.1 = ((s8[5767168]{0:T(1024)(128)(4,1)}), s8[4194304]{0:T(1024)(128)(4,1)S(1)}, s32[]{:S(2)}) async-start(s8[5767168]{0:T(1024)(128)(4,1)} %bitcast.224), calls=%async_computation.6 | async-start | bytes 8388608
  100.6 84.2 %slice-start.2 = ((s8[5767168]{0:T(1024)(128)(4,1)}), s8[1572864]{0:T(1024)(128)(4,1)S(1)}, s32[]{:S(2)}) async-start(s8[5767168]{0:T(1024)(128)(4,1)} %bitcast.224), calls=%async_computation.7 | async-start | bytes 3145728
  188.3 3.7 %copy-start.11 = (bf16[2,352,2048]{2,1,0:T(8,128)(2,1)S(1)}, bf16[2,352,2048]{2,1,0:T(8,128)(2,1)}, u32[]{:S(2)}) copy-start(bf16[2,352,2048]{2,1,0:T(8,128)(2,1)} %param.33) | copy-start | bytes 8650756
  201.7 5.5 %copy-start.10 = (s32[2]{0:T(128)S(1)}, s32[2]{0:T(128)}, u32[]{:S(2)}) copy-start(s32[2]{0:T(128)} %param.25) | copy-start | bytes 28
  201.7 5.8 %copy-start.2 = (s32[2,32]{1,0:T(2,128)S(1)}, s32[2,32]{1,0:T(2,128)}, u32[]{:S(2)}) copy-start(s32[2,32]{1,0:T(2,128)} %param.22) | copy-start | bytes 772
  201.7 11.0 %copy-start.15 = (bf16[2048,64]{0,1:T(8,128)(2,1)S(1)}, bf16[2048,64]{0,1:T(8,128)(2,1)}, u32[]{:S(2)}) copy-start(bf16[2048,64]{0,1:T(8,128)(2,1)} %param.30) | copy-start | bytes 786436
  201.7 80.4 %all-to-all-start.1 = ((bf16[128,2,24,512]{3,2,1,0:T(8,128)(2,1)}), bf16[128,2,24,512]{3,2,1,0:T(8,128)(2,1)}, u32[]{:S(2)}, u32[]{:S(2)}) async-start(bf16[128,2,24,512]{3,2,1,0:T(8,128)(2,1)} %bitcast.211), calls=%async_computation.2 | async-start | bytes 12582912 | tf_op jit(solution)/shard_map/all_to_all | solution.py:323
  206.9 81.0 %reduce-scatter.2.cloned.1.call-start = ((), (), s32[]{:S(2)}) async-start(), calls=%async_computation.3 | async-start | bytes 655360 | tf_op jit(solution)/shard_map/reduce_scatter | solution.py:341
  219.7 2.7 copy-start.12
  222.4 1.4 copy-start.14
  282.2 7.3 %copy-start.1 = (bf16[16,128,512]{2,1,0:T(8,128)(2,1)S(1)}, bf16[16,128,512]{2,1,0:T(8,128)(2,1)}, u32[]{:S(2)}) copy-start(bf16[16,128,512]{2,1,0:T(8,128)(2,1)} %param.26) | copy-start | bytes 6291460
Sparse Core Ops, SparseCore 0:
  49.1 35.0 all-gather.2
  227.6 53.9 reduce-scatter.1

commit v4 on v3

--- a/solution.py
+++ b/solution.py
@@ -115,7 +115,7 @@
     local_pages = slots.shape[1]
     page_size = cache_pool.shape[2]
     draft_pad = draft_rows.shape[1]
-    row_block = 256
+    row_block = 512
     kernel = functools.partial(
         attention_kernel,
         page_size=page_size,

time: 297 us -> 300 us (1.010); the launches traced: 296 us -> 296 us
  no operation moved by 1% of the time
where the time goes in v4:
time: 300 us; the launch traced here: 296 us
  blocking collectives  94.3 us (31%)
  waiting for transfers between devices  81.4 us (27%)
  matrix products  31.8 us (11%)
  local copies, waits for them, and re-layouts  26.8 us (9%)
  Pallas kernels  23.6 us (8%)
  other arithmetic  17.7 us (6%)
  between operations  15.2 us (5%)
  starting transfers between devices  5.2 us (2%)
    all_to_all x1, blocking collectives, per_device(): lax.all_to_all(outgoing, 'ep', split_axis=0, concat_axis=0, tiled=True)  84.4 us
    all_to_all x1, waiting for transfers between devices, per_device(): lax.all_to_all(sending, ('req', 'ep'), 0, 0, tiled=True)  49.8 us
    all_gather x1, waiting for transfers between devices, per_device(): gathered = lax.all_gather(packed, 'req').astype(jnp.float32)  31.6 us
    pallas_call x1, Pallas kernels, paged_attention(): pl.pallas_call(kernel, grid_spec=grid_spec, out_shape=[jax.ShapeDtypeStru...  23.6 us
    all_gather x1, blocking collectives, per_device(): resid = lax.all_gather(resid_cols, 'req', axis=1, tiled=True)  9.9 us
  transfers between devices with their start and end apart: 3, of which 2 were waited for; matrix products, arithmetic and copies ran while one was open for 11% of the time, Pallas kernels for 0%

profile of v4, /device:TPU:1, one launch (start us, length us, event | category | flops | bytes accessed | tf_op | source)
XLA Modules:
  0.0 296.1 jit_solution(2762342421735254835)
XLA Ops:
  7.3 0.9 copy.143
  8.2 0.6 gather_fusion
  8.8 1.8 convert_bitcast_fusion
  10.7 1.2 copy.146
  14.2 0.6 gather_fusion.1
  14.8 0.6 gather_fusion.2
  15.9 23.6 %shard_map.185 = (f32[2,1024,512]{2,1,0:T(8,128)}, f32[2,1024,128]{2,1,0:T(8,128)S(1)}) custom-call(s32[2,8]{1,0:T(2,128)S(1)} %clamp_bitcast_fusion.slots_ref, s32[2,8]{1,0:T(2,128)S(1)} %subtract_clamp_fusion.limits_ref, bf16[2,1024,512]{2,1,0:T(8,128)(2,1)S(1)} %bitcast.208, bf16[2,1024,64]{2,1,0:T(8,128)(2,1)S(1)} %bitcast.209, ...), custom_call_target="tpu_custom_call" | custom-call | flops 5133828096 | bytes 11010048 | tf_op jit(solution)/shard_map/pallas_call | solution.py:150
  39.6 2.6 convert_element_type.160
  42.4 2.5 fusion.44
  45.4 0.9 slice_reduce_fusion.1
  47.0 1.0 concatenate.19
  48.5 1.8 reduce-window.6
  50.9 0.8 fusion.4
  51.8 31.6 %all-gather.3.cloned.1.call-done = bf16[512,2144]{1,0:T(8,128)(2,1)} async-done(((bf16[128,2144]{1,0:T(8,128)(2,1)}), bf16[512,2144]{1,0:T(8,128)(2,1)}) %all-gather.3.cloned.1.call-update) | async-done | bytes 2195472 | tf_op jit(solution)/shard_map/all_gather | solution.py:243
  83.3 1.9 bitcast_convert_fusion
  85.7 0.8 fusion.5
  86.4 0.8 copy-done.3
  87.7 9.9 %all_gather.11 = bf16[128,2048]{1,0:T(8,128)(2,1)S(1)} all-gather(bf16[128,512]{1,0:T(8,128)(2,1)S(1)} %fusion.51), channel_id=1, replica_groups=mesh['req'=4,'ep'=32] {'req'}, dimensions={1}, use_global_device_ids=true | all-gather | bytes 655360 | tf_op jit(solution)/shard_map/all_gather | solution.py:266
  97.8 1.9 convolution_convert_fusion
  99.7 84.4 %all_to_all.10 = bf16[32,2,24,2048]{3,2,1,0:T(8,128)(2,1)S(1)} all-to-all(bf16[32,2,24,2048]{3,2,1,0:T(8,128)(2,1)S(1)} %bitcast.210), channel_id=1, replica_groups=mesh['req'=4,'ep'=32] {'ep'}, dimensions={0} | all-to-all | bytes 12582912 | tf_op jit(solution)/shard_map/all_to_all | solution.py:297
  184.2 3.5 %fusion.2 = f32[2,32,24,352]{3,2,1,0:T(8,128)S(1)} fusion(bf16[32,2,24,2048]{3,2,1,0:T(8,128)(2,1)S(1)} %all_to_all.10, bf16[2,2,2048,352]{2,3,1,0:T(8,128)(2,1)S(1)} %bitcast.225), kind=kOutput, calls=%fused_computation.11 | convolution fusion | flops 2214592512 | bytes 11337728 | tf_op jit(solution)/shard_map/pecd,edf->pecf/dot_general | solution.py:298
  187.6 3.7 %fusion.14 = bf16[32,2,24,352]{3,2,0,1:T(8,128)(2,1)S(1)} fusion(f32[2,32,24,352]{3,2,1,0:T(8,128)S(1)} %fusion.2, bf16[2,2,2048,352]{2,3,1,0:T(8,128)(2,1)S(1)} %bitcast.225, bf16[32,2,24,2048]{3,2,1,0:T(8,128)(2,1)S(1)} %all_to_all.10), kind=kOutput, calls=%fused_computation.30 | convolution fusion | flops 2217836544 | bytes 12615680 | tf_op jit(solution)/shard_map/pecd,edf->pecf/dot_general | solution.py:301
  191.3 0.6 fusion.36
  191.9 0.6 fusion.35
  192.5 0.6 fusion.38
  193.1 0.6 fusion.37
  193.7 0.6 fusion.32
  194.2 0.6 fusion.31
  194.8 0.6 fusion.34
  195.4 0.6 fusion.33
  196.6 0.8 pad_maximum_fusion
  197.4 3.6 %copy.173 = bf16[4,32,2,24,512]{4,3,2,1,0:T(8,128)(2,1)} copy(bf16[4,32,2,24,512]{4,3,1,2,0:T(8,128)(2,1)S(1)} %pad_maximum_fusion) | data formatting | bytes 12582912 | tf_op jit(solution)/shard_map/stack | solution.py:306
  201.0 5.1 %all-to-all-start.1 = ((bf16[128,2,24,512]{3,2,1,0:T(8,128)(2,1)}), bf16[128,2,24,512]{3,2,1,0:T(8,128)(2,1)}, u32[]{:S(2)}, u32[]{:S(2)}) async-start(bf16[128,2,24,512]{3,2,1,0:T(8,128)(2,1)} %bitcast.211), calls=%async_computation.2 | async-start | bytes 12582912 | tf_op jit(solution)/shard_map/all_to_all | solution.py:323
  206.8 0.6 gather_fusion.6
  207.5 2.3 gather_fusion.3
  210.1 0.6 gather_fusion.5
  210.9 1.1 fusion.50
  212.4 5.1 %gather_fusion.4 = f32[768]{0:T(1024)S(1)} fusion(f32[128,64]{0,1:T(8,128)S(1)} %fusion.125, s32[768]{0:T(1024)S(1)} %reshape.356), kind=kCustom, calls=%fused_computation.4 | custom fusion | bytes 12288 | tf_op jit(solution)/shard_map/jit(take_along_axis)/gather | solution.py:273
  217.7 0.7 select_reduce_fusion
  218.4 0.5 tile.4
  219.0 2.7 copy.188
  221.6 0.6 fusion.27
  222.3 0.7 copy-done.14
  223.0 3.7 %convolution_convert_fusion.1 = bf16[128,2048]{1,0:T(8,128)(2,1)} fusion(bf16[352,2048]{1,0:T(8,128)(2,1)S(1)} %copy-done.14, bf16[2,2048,352]{1,2,0:T(8,128)(2,1)} %param.34, f32[128,352]{0,1:T(8,128)S(1)} %fusion.27, bf16[128,2048]{1,0:T(8,128)(2,1)S(1)} %all_gather.11, f32[2048]{0:T(1024)S(1)} %copy-done.7, f32[128]{0:T(128)S(1)} %add_rsqrt_fusion), kind=kOutput, calls=%fused_computation.28 | convolution fusion | flops 370679808 | bytes 4121088 | tf_op jit(solution)/shard_map/dot_general | solution.py:278
  226.7 5.0 %subtract_convert_fusion = (bf16[128,6144]{1,0:T(8,128)(2,1)}, bf16[128,6144]{1,0:T(8,128)(2,1)}) fusion(f32[128,6144]{1,0:T(8,128)} %bitcast.212), kind=kLoop, calls=%fused_computation.23 | loop fusion | flops 3145728 | bytes 6291456 | tf_op jit(solution)/shard_map/convert_element_type | solution.py:334
  231.7 49.8 %all-to-all-done.1 = bf16[128,2,24,512]{3,2,1,0:T(8,128)(2,1)} async-done(((bf16[128,2,24,512]{3,2,1,0:T(8,128)(2,1)}), bf16[128,2,24,512]{3,2,1,0:T(8,128)(2,1)}, u32[]{:S(2)}, u32[]{:S(2)}) %all-to-all-start.1) | async-done | bytes 6291488 | tf_op jit(solution)/shard_map/all_to_all | solution.py:323
  281.5 5.7 %fusion.6 = f32[256,512]{1,0:T(8,128)S(1)} fusion(bf16[6144,512]{1,0:T(8,128)(2,1)} %bitcast.62, bf16[128,6144]{1,0:T(8,128)(2,1)} %get-tuple-element.20, bf16[128,6144]{1,0:T(8,128)(2,1)} %get-tuple-element.21), kind=kOutput, calls=%fused_computation.19 | convolution fusion | flops 1616904192 | bytes 9961472 | tf_op jit(solution)/shard_map/dot_general | solution.py:335
  287.2 1.6 fusion.82
  (123 shorter events, 8.8 us)
Async XLA Ops:
  7.2 1.7 copy-start
  7.2 76.1 %all-gather.3.cloned.1.call-start = ((), (), s32[]{:S(2)}) async-start(), calls=%async_computation.4 | async-start | bytes 2785280 | tf_op jit(solution)/shard_map/all_gather | solution.py:243
  10.7 1.2 slice-start
  10.7 1.7 copy-start.4
  10.7 2.0 copy-start.9
  11.9 3.8 %copy-start.8 = (s32[2]{0:T(128)S(1)}, s32[2]{0:T(128)}, u32[]{:S(2)}) copy-start(s32[2]{0:T(128)} %param.23) | copy-start | bytes 28
  39.6 2.9 copy-start.13
  45.4 2.7 copy-start.6
  85.7 1.6 copy-start.3
  85.7 1.6 copy-start.5
  87.3 10.6 %copy-start.7 = (f32[2048]{0:T(1024)S(1)}, f32[2048]{0:T(1024)}, u32[]{:S(2)}) copy-start(f32[2048]{0:T(1024)} %param.29) | copy-start | bytes 24580
  97.8 86.3 %slice-start.1 = ((s8[5767168]{0:T(1024)(128)(4,1)}), s8[4194304]{0:T(1024)(128)(4,1)S(1)}, s32[]{:S(2)}) async-start(s8[5767168]{0:T(1024)(128)(4,1)} %bitcast.224), calls=%async_computation.6 | async-start | bytes 8388608
  99.7 84.5 %slice-start.2 = ((s8[5767168]{0:T(1024)(128)(4,1)}), s8[1572864]{0:T(1024)(128)(4,1)S(1)}, s32[]{:S(2)}) async-start(s8[5767168]{0:T(1024)(128)(4,1)} %bitcast.224), calls=%async_computation.7 | async-start | bytes 3145728
  187.6 3.7 %copy-start.11 = (bf16[2,352,2048]{2,1,0:T(8,128)(2,1)S(1)}, bf16[2,352,2048]{2,1,0:T(8,128)(2,1)}, u32[]{:S(2)}) copy-start(bf16[2,352,2048]{2,1,0:T(8,128)(2,1)} %param.33) | copy-start | bytes 8650756
  201.0 5.5 %copy-start.10 = (s32[2]{0:T(128)S(1)}, s32[2]{0:T(128)}, u32[]{:S(2)}) copy-start(s32[2]{0:T(128)} %param.25) | copy-start | bytes 28
  201.0 5.8 %copy-start.2 = (s32[2,32]{1,0:T(2,128)S(1)}, s32[2,32]{1,0:T(2,128)}, u32[]{:S(2)}) copy-start(s32[2,32]{1,0:T(2,128)} %param.22) | copy-start | bytes 772
  201.0 10.9 %copy-start.15 = (bf16[2048,64]{0,1:T(8,128)(2,1)S(1)}, bf16[2048,64]{0,1:T(8,128)(2,1)}, u32[]{:S(2)}) copy-start(bf16[2048,64]{0,1:T(8,128)(2,1)} %param.30) | copy-start | bytes 786436
  201.0 80.5 %all-to-all-start.1 = ((bf16[128,2,24,512]{3,2,1,0:T(8,128)(2,1)}), bf16[128,2,24,512]{3,2,1,0:T(8,128)(2,1)}, u32[]{:S(2)}, u32[]{:S(2)}) async-start(bf16[128,2,24,512]{3,2,1,0:T(8,128)(2,1)} %bitcast.211), calls=%async_computation.2 | async-start | bytes 12582912 | tf_op jit(solution)/shard_map/all_to_all | solution.py:323
  206.2 81.0 %reduce-scatter.2.cloned.1.call-start = ((), (), s32[]{:S(2)}) async-start(), calls=%async_computation.3 | async-start | bytes 655360 | tf_op jit(solution)/shard_map/reduce_scatter | solution.py:341
  219.0 2.7 copy-start.12
  221.6 1.4 copy-start.14
  281.5 7.3 %copy-start.1 = (bf16[16,128,512]{2,1,0:T(8,128)(2,1)S(1)}, bf16[16,128,512]{2,1,0:T(8,128)(2,1)}, u32[]{:S(2)}) copy-start(bf16[16,128,512]{2,1,0:T(8,128)(2,1)} %param.26) | copy-start | bytes 6291460
Sparse Core Ops, SparseCore 0:
  48.2 35.1 all-gather.2
  226.8 54.0 reduce-scatter.1
